TPU v7x, 128 devices: a whole 4x4x4 slice. The times are simulated.
128 devices in a mesh: month: 4 (over x), grid: 32 (over y, z, core).
Axes of the slice: x: 4, y: 4, z: 4, core: 2. Of those that a mesh axis runs over, the one named last changes fastest.
Arguments:
- tracers: float32 [64, 32768], P(None, 'grid'), may hold values from 0.25 to 7
- targets: float32 [64], replicated, may hold values from 0.5 to 2
- retain: float32 [8, 32768], P('month', 'grid'), may hold values from 0.5 to 0.95
- blocks: float32 [8, 256, 8, 128, 128], P('month', 'grid'), may hold values from 3.90625e-07 to 0.00390625
- cols: int32 [8, 256, 8], P('month', 'grid'), may hold values from 0 to 255, as said below
Outputs:
- spun_up: float32 [64, 32768], P('month', 'grid')
Inputs may be any that keep to these rules, and one draw needn't show every extreme that they name: cols[m, i, 0] = i; for 1 <= k < 6, cols[m, i, k] names a block on the same grid device as block i (block b lies on device b // 8); the last 2 entries name blocks on other devices, and of the 16 such entries of one device's block rows in one month at most 1 lie on any single device, exactly 1 on some.
All inputs are finite; a program needn't handle non-finite values.
Results may differ from a plain program's by a relative error of at most 0.0001.
Values sent between devices are 32-bit elements; how exact they have to be, the bound alone decides.
No kernel may reach another device: no remote copies, remote signals or barrier semaphores. Data moves between devices by JAX's collectives and lax.ppermute only.
A program may use at most 64 MiB of HBM per device.

v0:
```python
import jax
import jax.numpy as jnp
from jax import lax
from jax.sharding import PartitionSpec as P


def passed_along(value, axis, by):
    devices = lax.axis_size(axis)
    return lax.ppermute(value, axis, [(i, (i + by) % devices) for i in range(devices)])


def local(tracers, targets, retain, blocks, cols):
    sections = lax.axis_size("month")
    devices = lax.axis_size("grid")
    section = lax.axis_index("month")
    months_here = blocks.shape[0]
    blk_count = blocks.shape[1]
    blk_size = blocks.shape[3]
    rows_here = blk_count * blk_size
    batch = tracers.shape[0] // sections
    points = rows_here * devices
    held = jnp.zeros((batch, rows_here), jnp.float32)
    kept = jnp.zeros((batch, rows_here), jnp.float32)
    last_step = max(2 * sections - 2, 3 * sections - 4)
    for step in range(last_step + 1):
        if step < sections:
            held = jnp.where(section == 0, tracers[step * batch : (step + 1) * batch], held)
        if step < 2 * sections - 1:
            working = (step - section >= 0) & (step - section < sections)
            apply_state = held
            for apply_month_idx in range(months_here):
                whole = lax.all_gather(apply_state, "grid", axis=1, tiled=True)
                picked = whole.reshape(batch, -1, blk_size)[:, cols[apply_month_idx]]
                mixed = jnp.einsum(
                    "tbkc,bkrc->tbr",
                    picked,
                    blocks[apply_month_idx],
                    precision=lax.Precision.HIGHEST,
                    preferred_element_type=jnp.float32,
                )
                apply_state = retain[apply_month_idx][None, :] * apply_state + mixed.reshape(
                    batch, rows_here
                )
            held = jnp.where(working, apply_state, held)
            finished = step - sections + 1
            if finished >= 0:
                inventory = lax.psum(jnp.sum(held, axis=1), "grid")
                goal = targets[finished * batch : (finished + 1) * batch]
                scaled = held * (goal * points / inventory)[:, None]
                held = jnp.where(section == sections - 1, scaled, held)
        arrived = jnp.where(
            section == sections - 1, step == 2 * sections - 2, step == sections + 2 * section
        )
        kept = jnp.where(arrived, held, kept)
        if step < last_step:
            held = passed_along(held, "month", 1)
    return kept


def solution(mesh):
    return jax.shard_map(
        local,
        mesh=mesh,
        in_specs=(
            P(None, "grid"),
            P(),
            P("month", "grid"),
            P("month", "grid", None, None, None),
            P("month", "grid", None),
        ),
        out_specs=P("month", "grid"),
        check_vma=False,
    )
```

profile of v0, /device:TPU:0, one launch (start us, length us, event | category | flops | bytes accessed | tf_op | source)
XLA Modules:
  0.0 1031.2 jit_solution(10049208585597531722)
XLA Ops:
  9.7 46.3 %all-gather.15.cloned.1.call-done = f32[16,32768]{1,0:T(8,128)} async-done(((f32[16,1024]{1,0:T(8,128)}), f32[16,32768]{1,0:T(8,128)}) %all-gather.15.cloned.1.call-update) | async-done | bytes 2097168 | tf_op jit(solution)/shard_map/all_gather | solution.py:32
  58.4 5.3 fusion.42
  64.6 43.0 %all-gather.17.cloned.1.call-done = f32[16,32768]{1,0:T(8,128)} async-done(((f32[16,1024]{1,0:T(8,128)}), f32[16,32768]{1,0:T(8,128)}) %all-gather.17.cloned.1.call-update) | async-done | bytes 2097168 | tf_op jit(solution)/shard_map/all_gather | solution.py:32
  110.0 5.3 fusion.63
  121.6 41.9 %all-gather.19.cloned.1.call-done = f32[16,32768]{1,0:T(8,128)} async-done(((f32[16,1024]{1,0:T(8,128)}), f32[16,32768]{1,0:T(8,128)}) %all-gather.19.cloned.1.call-update) | async-done | bytes 2097168 | tf_op jit(solution)/shard_map/all_gather | solution.py:32
  172.0 43.1 %all-gather.21.cloned.1.call-done = f32[16,32768]{1,0:T(8,128)} async-done(((f32[16,1024]{1,0:T(8,128)}), f32[16,32768]{1,0:T(8,128)}) %all-gather.21.cloned.1.call-update) | async-done | bytes 2097168 | tf_op jit(solution)/shard_map/all_gather | solution.py:32
  217.5 5.3 fusion.66
  229.2 41.9 %all-gather.23.cloned.1.call-done = f32[16,32768]{1,0:T(8,128)} async-done(((f32[16,1024]{1,0:T(8,128)}), f32[16,32768]{1,0:T(8,128)}) %all-gather.23.cloned.1.call-update) | async-done | bytes 2097168 | tf_op jit(solution)/shard_map/all_gather | solution.py:32
  279.7 42.9 %all-gather.25.cloned.1.call-done = f32[16,32768]{1,0:T(8,128)} async-done(((f32[16,1024]{1,0:T(8,128)}), f32[16,32768]{1,0:T(8,128)}) %all-gather.25.cloned.1.call-update) | async-done | bytes 2097168 | tf_op jit(solution)/shard_map/all_gather | solution.py:32
  325.1 5.3 fusion.69
  336.7 41.9 %all-gather.27.cloned.1.call-done = f32[16,32768]{1,0:T(8,128)} async-done(((f32[16,1024]{1,0:T(8,128)}), f32[16,32768]{1,0:T(8,128)}) %all-gather.27.cloned.1.call-update) | async-done | bytes 2097168 | tf_op jit(solution)/shard_map/all_gather | solution.py:32
  387.1 43.1 %all-gather.29.cloned.1.call-done = f32[16,32768]{1,0:T(8,128)} async-done(((f32[16,1024]{1,0:T(8,128)}), f32[16,32768]{1,0:T(8,128)}) %all-gather.29.cloned.1.call-update) | async-done | bytes 2097168 | tf_op jit(solution)/shard_map/all_gather | solution.py:32
  438.1 65.2 %psum.28 = f32[16]{0:T(128)S(1)} all-reduce(f32[16]{0:T(128)S(1)} %get-tuple-element.11), channel_id=1, replica_groups=mesh['month'=4,'grid'=32] {'grid'}, use_global_device_ids=true, to_apply=%region_1.2 | all-reduce | flops 16 | bytes 128 | tf_op jit(solution)/shard_map/psum | solution.py:47
  509.5 38.9 %all-gather.31.cloned.1.call-done = f32[16,32768]{1,0:T(8,128)} async-done(((f32[16,1024]{1,0:T(8,128)}), f32[16,32768]{1,0:T(8,128)}) %all-gather.31.cloned.1.call-update) | async-done | bytes 2097168 | tf_op jit(solution)/shard_map/all_gather | solution.py:32
  556.9 43.1 %all-gather.33.cloned.1.call-done = f32[16,32768]{1,0:T(8,128)} async-done(((f32[16,1024]{1,0:T(8,128)}), f32[16,32768]{1,0:T(8,128)}) %all-gather.33.cloned.1.call-update) | async-done | bytes 2097168 | tf_op jit(solution)/shard_map/all_gather | solution.py:32
  607.9 65.2 %psum.29 = f32[16]{0:T(128)S(1)} all-reduce(f32[16]{0:T(128)S(1)} %get-tuple-element.9), channel_id=1, replica_groups=mesh['month'=4,'grid'=32] {'grid'}, use_global_device_ids=true, to_apply=%region_3.4 | all-reduce | flops 16 | bytes 128 | tf_op jit(solution)/shard_map/psum | solution.py:47
  679.6 38.7 %all-gather.35.cloned.1.call-done = f32[16,32768]{1,0:T(8,128)} async-done(((f32[16,1024]{1,0:T(8,128)}), f32[16,32768]{1,0:T(8,128)}) %all-gather.35.cloned.1.call-update) | async-done | bytes 2097168 | tf_op jit(solution)/shard_map/all_gather | solution.py:32
  726.8 43.1 %all-gather.37.cloned.1.call-done = f32[16,32768]{1,0:T(8,128)} async-done(((f32[16,1024]{1,0:T(8,128)}), f32[16,32768]{1,0:T(8,128)}) %all-gather.37.cloned.1.call-update) | async-done | bytes 2097168 | tf_op jit(solution)/shard_map/all_gather | solution.py:32
  772.3 5.3 fusion.78
  777.8 65.2 %psum.30 = f32[16]{0:T(128)S(1)} all-reduce(f32[16]{0:T(128)S(1)} %get-tuple-element.7), channel_id=1, replica_groups=mesh['month'=4,'grid'=32] {'grid'}, use_global_device_ids=true, to_apply=%region_5.6 | all-reduce | flops 16 | bytes 128 | tf_op jit(solution)/shard_map/psum | solution.py:47
  849.3 38.9 %all-gather.39.cloned.1.call-done = f32[16,32768]{1,0:T(8,128)} async-done(((f32[16,1024]{1,0:T(8,128)}), f32[16,32768]{1,0:T(8,128)}) %all-gather.39.cloned.1.call-update) | async-done | bytes 2097168 | tf_op jit(solution)/shard_map/all_gather | solution.py:32
  896.6 43.2 %all-gather.41.cloned.1.call-done = f32[16,32768]{1,0:T(8,128)} async-done(((f32[16,1024]{1,0:T(8,128)}), f32[16,32768]{1,0:T(8,128)}) %all-gather.41.cloned.1.call-update) | async-done | bytes 2097168 | tf_op jit(solution)/shard_map/all_gather | solution.py:32
  942.2 5.3 fusion.81
  947.6 65.2 %psum.31 = f32[16]{0:T(128)S(1)} all-reduce(f32[16]{0:T(128)S(1)} %get-tuple-element.5), channel_id=1, replica_groups=mesh['month'=4,'grid'=32] {'grid'}, use_global_device_ids=true, to_apply=%region_7.8 | all-reduce | flops 16 | bytes 128 | tf_op jit(solution)/shard_map/psum | solution.py:47
  (149 shorter events, 134.6 us)
Async XLA Ops:
  6.5 49.5 %all-gather.15.cloned.1.call-start = ((), (), s32[]{:S(2)}) async-start(), calls=%async_computation | async-start | bytes 2162688 | tf_op jit(solution)/shard_map/all_gather | solution.py:32
  8.0 99.6 %all-gather.17.cloned.1.call-start = ((), (), s32[]{:S(2)}) async-start(), calls=%async_computation.1 | async-start | bytes 2162688 | tf_op jit(solution)/shard_map/all_gather | solution.py:32
  58.4 5.3 copy-start.3
  64.4 99.1 %all-gather.19.cloned.1.call-start = ((), (), s32[]{:S(2)}) async-start(), calls=%async_computation.2 | async-start | bytes 2162688 | tf_op jit(solution)/shard_map/all_gather | solution.py:32
  115.4 5.5 collective-permute-start
  121.6 93.6 %all-gather.21.cloned.1.call-start = ((), (), s32[]{:S(2)}) async-start(), calls=%async_computation.3 | async-start | bytes 2162688 | tf_op jit(solution)/shard_map/all_gather | solution.py:32
  172.0 99.1 %all-gather.23.cloned.1.call-start = ((), (), s32[]{:S(2)}) async-start(), calls=%async_computation.4 | async-start | bytes 2162688 | tf_op jit(solution)/shard_map/all_gather | solution.py:32
  222.9 5.5 collective-permute-start.1
  229.1 93.6 %all-gather.25.cloned.1.call-start = ((), (), s32[]{:S(2)}) async-start(), calls=%async_computation.5 | async-start | bytes 2162688 | tf_op jit(solution)/shard_map/all_gather | solution.py:32
  279.5 99.1 %all-gather.27.cloned.1.call-start = ((), (), s32[]{:S(2)}) async-start(), calls=%async_computation.6 | async-start | bytes 2162688 | tf_op jit(solution)/shard_map/all_gather | solution.py:32
  330.4 5.5 collective-permute-start.2
  336.7 93.6 %all-gather.29.cloned.1.call-start = ((), (), s32[]{:S(2)}) async-start(), calls=%async_computation.7 | async-start | bytes 2162688 | tf_op jit(solution)/shard_map/all_gather | solution.py:32
  387.0 161.4 %all-gather.31.cloned.1.call-start = ((), (), s32[]{:S(2)}) async-start(), calls=%async_computation.8 | async-start | bytes 2162688 | tf_op jit(solution)/shard_map/all_gather | solution.py:32
  432.6 70.6 %copy-start.17 = (f32[64]{0:T(128)S(1)}, f32[64]{0:T(128)}, u32[]{:S(2)}) copy-start(f32[64]{0:T(128)} %param.6) | copy-start | bytes 772
  503.3 5.5 collective-permute-start.3
  509.5 90.5 %all-gather.33.cloned.1.call-start = ((), (), s32[]{:S(2)}) async-start(), calls=%async_computation.9 | async-start | bytes 2162688 | tf_op jit(solution)/shard_map/all_gather | solution.py:32
  556.8 161.5 %all-gather.35.cloned.1.call-start = ((), (), s32[]{:S(2)}) async-start(), calls=%async_computation.10 | async-start | bytes 2162688 | tf_op jit(solution)/shard_map/all_gather | solution.py:32
  673.2 5.5 collective-permute-start.4
  679.4 90.5 %all-gather.37.cloned.1.call-start = ((), (), s32[]{:S(2)}) async-start(), calls=%async_computation.11 | async-start | bytes 2162688 | tf_op jit(solution)/shard_map/all_gather | solution.py:32
  726.7 161.5 %all-gather.39.cloned.1.call-start = ((), (), s32[]{:S(2)}) async-start(), calls=%async_computation.12 | async-start | bytes 2162688 | tf_op jit(solution)/shard_map/all_gather | solution.py:32
  843.1 5.5 collective-permute-start.5
  849.2 90.5 %all-gather.41.cloned.1.call-start = ((), (), s32[]{:S(2)}) async-start(), calls=%async_computation.13 | async-start | bytes 2162688 | tf_op jit(solution)/shard_map/all_gather | solution.py:32
  1013.0 5.5 collective-permute-start.6
  1018.5 5.5 collective-permute-start.7
  (16 other events, 71.2 us)
Sparse Core Ops, SparseCore 0:
  9.7 46.2 all-gather.14
  64.5 43.0 all-gather.16
  121.7 41.8 all-gather.18
  172.1 43.0 all-gather.20
  229.2 41.8 all-gather.22
  279.6 43.0 all-gather.24
  336.8 41.8 all-gather.26
  387.2 43.0 all-gather.28
  509.6 38.7 all-gather.30
  557.0 43.0 all-gather.32
  679.5 38.7 all-gather.34
  726.8 43.0 all-gather.36
  849.4 38.7 all-gather.38
  896.7 43.0 all-gather.40
where the time goes:
time: 1030 us
  waiting for transfers between devices  623 us (60%)
  blocking collectives  261 us (25%)
  matrix products  74.5 us (7%)
  local copies, waits for them, and re-layouts  36.2 us (4%)
  between operations  13.7 us (1%)
  starting transfers between devices  12 us (1%)
  other arithmetic  10.6 us (1%)
    all_gather x14, waiting for transfers between devices, local(): whole = lax.all_gather(apply_state, 'grid', axis=1, tiled=True)  590 us
    psum x4, blocking collectives, local(): inventory = lax.psum(jnp.sum(held, axis=1), 'grid')  261 us
    dot_general x14, matrix products, local(): jnp.einsum('tbkc,bkrc->tbr', picked, blocks[apply_month_idx], precision=l...  74.5 us
    ppermute x8, waiting for transfers between devices, passed_along(): lax.ppermute(value, axis, [(i, (i + by) % devices) for i in range(devices)])  33 us
    reshape x14, local copies, waits for them, and re-layouts, local(): picked = whole.reshape(batch, -1, blk_size)[:, cols[apply_month_idx]]  24.5 us
  transfers between devices with their start and end apart: 22, of which 22 were waited for; matrix products, arithmetic and copies ran while one was open for 0% of the time, Pallas kernels for 0%

commit v1 on v0

--- a/solution.py
+++ b/solution.py
@@ -1,7 +1,16 @@
+import functools
 import jax
 import jax.numpy as jnp
 from jax import lax
 from jax.sharding import PartitionSpec as P
+
+
+def produce_the_face(x0, row_axis):
+    local_next = jnp.sum(lax.all_gather(x0, row_axis), 0)
+    return local_next
+
+
+lift_waves = functools.partial(produce_the_face, row_axis="grid")
 
 
 def passed_along(value, axis, by):
@@ -44,7 +53,7 @@
             held = jnp.where(working, apply_state, held)
             finished = step - sections + 1
             if finished >= 0:
-                inventory = lax.psum(jnp.sum(held, axis=1), "grid")
+                inventory = lift_waves(jnp.sum(held, axis=1))
                 goal = targets[finished * batch : (finished + 1) * batch]
                 scaled = held * (goal * points / inventory)[:, None]
                 held = jnp.where(section == sections - 1, scaled, held)

time: 1030 us -> 1030 us (level)
    psum x4 -> x0, blocking collectives: 261 us -> none  [local(): inventory = lax.psum(jnp.sum(held, axis=1), 'grid')]
    unnamed x0 -> x4, blocking collectives: none -> 261 us
where the time goes in v1:
time: 1030 us
  waiting for transfers between devices  622 us (60%)
  blocking collectives  261 us (25%)
  matrix products  74.5 us (7%)
  local copies, waits for them, and re-layouts  38.2 us (4%)
  between operations  14.5 us (1%)
  starting transfers between devices  12 us (1%)
  other arithmetic  10.7 us (1%)
    all_gather x14, waiting for transfers between devices, local(): whole = lax.all_gather(apply_state, 'grid', axis=1, tiled=True)  589 us
    unnamed x4, blocking collectives  261 us
    dot_general x14, matrix products, local(): jnp.einsum('tbkc,bkrc->tbr', picked, blocks[apply_month_idx], precision=l...  74.5 us
    ppermute x8, waiting for transfers between devices, passed_along(): lax.ppermute(value, axis, [(i, (i + by) % devices) for i in range(devices)])  33 us
    reshape x14, local copies, waits for them, and re-layouts, local(): picked = whole.reshape(batch, -1, blk_size)[:, cols[apply_month_idx]]  24.5 us
  transfers between devices with their start and end apart: 22, of which 22 were waited for; matrix products, arithmetic and copies ran while one was open for 0% of the time, Pallas kernels for 0%

profile of v1, /device:TPU:0, one launch (start us, length us, event | category | flops | bytes accessed | tf_op | source)
XLA Modules:
  0.0 1032.6 jit_solution(3975576434973537787)
XLA Ops:
  9.7 46.3 %all-gather.19.cloned.1.call-done = f32[16,32768]{1,0:T(8,128)} async-done(((f32[16,1024]{1,0:T(8,128)}), f32[16,32768]{1,0:T(8,128)}) %all-gather.19.cloned.1.call-update) | async-done | bytes 2097168 | tf_op jit(solution)/shard_map/all_gather | solution.py:41
  58.4 5.3 fusion.42
  64.6 43.0 %all-gather.21.cloned.1.call-done = f32[16,32768]{1,0:T(8,128)} async-done(((f32[16,1024]{1,0:T(8,128)}), f32[16,32768]{1,0:T(8,128)}) %all-gather.21.cloned.1.call-update) | async-done | bytes 2097168 | tf_op jit(solution)/shard_map/all_gather | solution.py:41
  110.0 5.3 fusion.63
  121.6 41.9 %all-gather.23.cloned.1.call-done = f32[16,32768]{1,0:T(8,128)} async-done(((f32[16,1024]{1,0:T(8,128)}), f32[16,32768]{1,0:T(8,128)}) %all-gather.23.cloned.1.call-update) | async-done | bytes 2097168 | tf_op jit(solution)/shard_map/all_gather | solution.py:41
  172.0 43.1 %all-gather.25.cloned.1.call-done = f32[16,32768]{1,0:T(8,128)} async-done(((f32[16,1024]{1,0:T(8,128)}), f32[16,32768]{1,0:T(8,128)}) %all-gather.25.cloned.1.call-update) | async-done | bytes 2097168 | tf_op jit(solution)/shard_map/all_gather | solution.py:41
  217.5 5.3 fusion.66
  229.2 41.9 %all-gather.27.cloned.1.call-done = f32[16,32768]{1,0:T(8,128)} async-done(((f32[16,1024]{1,0:T(8,128)}), f32[16,32768]{1,0:T(8,128)}) %all-gather.27.cloned.1.call-update) | async-done | bytes 2097168 | tf_op jit(solution)/shard_map/all_gather | solution.py:41
  279.7 42.9 %all-gather.29.cloned.1.call-done = f32[16,32768]{1,0:T(8,128)} async-done(((f32[16,1024]{1,0:T(8,128)}), f32[16,32768]{1,0:T(8,128)}) %all-gather.29.cloned.1.call-update) | async-done | bytes 2097168 | tf_op jit(solution)/shard_map/all_gather | solution.py:41
  325.1 5.3 fusion.69
  336.7 41.9 %all-gather.31.cloned.1.call-done = f32[16,32768]{1,0:T(8,128)} async-done(((f32[16,1024]{1,0:T(8,128)}), f32[16,32768]{1,0:T(8,128)}) %all-gather.31.cloned.1.call-update) | async-done | bytes 2097168 | tf_op jit(solution)/shard_map/all_gather | solution.py:41
  388.4 41.8 %all-gather.33.cloned.1.call-done = f32[16,32768]{1,0:T(8,128)} async-done(((f32[16,1024]{1,0:T(8,128)}), f32[16,32768]{1,0:T(8,128)}) %all-gather.33.cloned.1.call-update) | async-done | bytes 2097168 | tf_op jit(solution)/shard_map/all_gather | solution.py:41
  438.3 65.1 %all-reduce = f32[512]{0:T(512)S(1)} all-reduce(f32[512]{0:T(512)S(1)} %dynamic-update-slice), channel_id=2, replica_groups=mesh['month'=4,'grid'=32] {'grid'}, use_global_device_ids=true, to_apply=%add | all-reduce | flops 512 | bytes 4096
  509.9 38.9 %all-gather.35.cloned.1.call-done = f32[16,32768]{1,0:T(8,128)} async-done(((f32[16,1024]{1,0:T(8,128)}), f32[16,32768]{1,0:T(8,128)}) %all-gather.35.cloned.1.call-update) | async-done | bytes 2097168 | tf_op jit(solution)/shard_map/all_gather | solution.py:41
  557.2 43.1 %all-gather.37.cloned.1.call-done = f32[16,32768]{1,0:T(8,128)} async-done(((f32[16,1024]{1,0:T(8,128)}), f32[16,32768]{1,0:T(8,128)}) %all-gather.37.cloned.1.call-update) | async-done | bytes 2097168 | tf_op jit(solution)/shard_map/all_gather | solution.py:41
  602.8 5.3 fusion.75
  608.5 65.1 %all-reduce.1 = f32[512]{0:T(512)S(1)} all-reduce(f32[512]{0:T(512)S(1)} %dynamic-update-slice.1), channel_id=3, replica_groups=mesh['month'=4,'grid'=32] {'grid'}, use_global_device_ids=true, to_apply=%add.1 | all-reduce | flops 512 | bytes 4096
  680.3 38.7 %all-gather.39.cloned.1.call-done = f32[16,32768]{1,0:T(8,128)} async-done(((f32[16,1024]{1,0:T(8,128)}), f32[16,32768]{1,0:T(8,128)}) %all-gather.39.cloned.1.call-update) | async-done | bytes 2097168 | tf_op jit(solution)/shard_map/all_gather | solution.py:41
  727.5 43.1 %all-gather.41.cloned.1.call-done = f32[16,32768]{1,0:T(8,128)} async-done(((f32[16,1024]{1,0:T(8,128)}), f32[16,32768]{1,0:T(8,128)}) %all-gather.41.cloned.1.call-update) | async-done | bytes 2097168 | tf_op jit(solution)/shard_map/all_gather | solution.py:41
  773.0 5.3 fusion.78
  778.7 65.1 %all-reduce.2 = f32[512]{0:T(512)S(1)} all-reduce(f32[512]{0:T(512)S(1)} %dynamic-update-slice.2), channel_id=4, replica_groups=mesh['month'=4,'grid'=32] {'grid'}, use_global_device_ids=true, to_apply=%add.2 | all-reduce | flops 512 | bytes 4096
  850.3 38.9 %all-gather.43.cloned.1.call-done = f32[16,32768]{1,0:T(8,128)} async-done(((f32[16,1024]{1,0:T(8,128)}), f32[16,32768]{1,0:T(8,128)}) %all-gather.43.cloned.1.call-update) | async-done | bytes 2097168 | tf_op jit(solution)/shard_map/all_gather | solution.py:41
  897.6 43.2 %all-gather.45.cloned.1.call-done = f32[16,32768]{1,0:T(8,128)} async-done(((f32[16,1024]{1,0:T(8,128)}), f32[16,32768]{1,0:T(8,128)}) %all-gather.45.cloned.1.call-update) | async-done | bytes 2097168 | tf_op jit(solution)/shard_map/all_gather | solution.py:41
  948.9 65.1 %all-reduce.3 = f32[512]{0:T(512)S(1)} all-reduce(f32[512]{0:T(512)S(1)} %dynamic-update-slice.3), channel_id=5, replica_groups=mesh['month'=4,'grid'=32] {'grid'}, use_global_device_ids=true, to_apply=%add.3 | all-reduce | flops 512 | bytes 4096
  (168 shorter events, 136.7 us)
Async XLA Ops:
  6.5 49.5 %all-gather.19.cloned.1.call-start = ((), (), s32[]{:S(2)}) async-start(), calls=%async_computation | async-start | bytes 2162688 | tf_op jit(solution)/shard_map/all_gather | solution.py:41
  8.0 99.6 %all-gather.21.cloned.1.call-start = ((), (), s32[]{:S(2)}) async-start(), calls=%async_computation.1 | async-start | bytes 2162688 | tf_op jit(solution)/shard_map/all_gather | solution.py:41
  64.4 99.1 %all-gather.23.cloned.1.call-start = ((), (), s32[]{:S(2)}) async-start(), calls=%async_computation.2 | async-start | bytes 2162688 | tf_op jit(solution)/shard_map/all_gather | solution.py:41
  115.4 5.5 collective-permute-start
  121.6 93.6 %all-gather.25.cloned.1.call-start = ((), (), s32[]{:S(2)}) async-start(), calls=%async_computation.3 | async-start | bytes 2162688 | tf_op jit(solution)/shard_map/all_gather | solution.py:41
  172.0 99.1 %all-gather.27.cloned.1.call-start = ((), (), s32[]{:S(2)}) async-start(), calls=%async_computation.4 | async-start | bytes 2162688 | tf_op jit(solution)/shard_map/all_gather | solution.py:41
  222.9 5.5 collective-permute-start.1
  229.1 93.6 %all-gather.29.cloned.1.call-start = ((), (), s32[]{:S(2)}) async-start(), calls=%async_computation.5 | async-start | bytes 2162688 | tf_op jit(solution)/shard_map/all_gather | solution.py:41
  279.5 99.1 %all-gather.31.cloned.1.call-start = ((), (), s32[]{:S(2)}) async-start(), calls=%async_computation.6 | async-start | bytes 2162688 | tf_op jit(solution)/shard_map/all_gather | solution.py:41
  330.4 5.5 collective-permute-start.2
  336.7 93.6 %all-gather.33.cloned.1.call-start = ((), (), s32[]{:S(2)}) async-start(), calls=%async_computation.7 | async-start | bytes 2162688 | tf_op jit(solution)/shard_map/all_gather | solution.py:41
  381.0 6.1 copy-start.18
  387.0 161.7 %all-gather.35.cloned.1.call-start = ((), (), s32[]{:S(2)}) async-start(), calls=%async_computation.8 | async-start | bytes 2162688 | tf_op jit(solution)/shard_map/all_gather | solution.py:41
  432.6 71.0 %copy-start.17 = (f32[64]{0:T(128)S(1)}, f32[64]{0:T(128)}, u32[]{:S(2)}) copy-start(f32[64]{0:T(128)} %param.6) | copy-start | bytes 772
  503.7 5.5 collective-permute-start.3
  509.8 90.5 %all-gather.37.cloned.1.call-start = ((), (), s32[]{:S(2)}) async-start(), calls=%async_computation.9 | async-start | bytes 2162688 | tf_op jit(solution)/shard_map/all_gather | solution.py:41
  557.2 161.8 %all-gather.39.cloned.1.call-start = ((), (), s32[]{:S(2)}) async-start(), calls=%async_computation.10 | async-start | bytes 2162688 | tf_op jit(solution)/shard_map/all_gather | solution.py:41
  673.9 5.5 collective-permute-start.4
  680.0 90.5 %all-gather.41.cloned.1.call-start = ((), (), s32[]{:S(2)}) async-start(), calls=%async_computation.11 | async-start | bytes 2162688 | tf_op jit(solution)/shard_map/all_gather | solution.py:41
  727.4 161.8 %all-gather.43.cloned.1.call-start = ((), (), s32[]{:S(2)}) async-start(), calls=%async_computation.12 | async-start | bytes 2162688 | tf_op jit(solution)/shard_map/all_gather | solution.py:41
  844.1 5.5 collective-permute-start.5
  850.3 90.5 %all-gather.45.cloned.1.call-start = ((), (), s32[]{:S(2)}) async-start(), calls=%async_computation.13 | async-start | bytes 2162688 | tf_op jit(solution)/shard_map/all_gather | solution.py:41
  1014.3 5.5 collective-permute-start.6
  1019.8 5.5 collective-permute-start.7
  (17 other events, 76.6 us)
Sparse Core Ops, SparseCore 0:
  9.7 46.2 all-gather.18
  64.5 43.0 all-gather.20
  121.7 41.8 all-gather.22
  172.1 43.0 all-gather.24
  229.2 41.8 all-gather.26
  279.6 43.0 all-gather.28
  336.8 41.8 all-gather.30
  387.2 43.0 all-gather.32
  509.9 38.7 all-gather.34
  557.3 43.0 all-gather.36
  680.2 38.7 all-gather.38
  727.5 43.0 all-gather.40
  850.4 38.7 all-gather.42
  897.8 43.0 all-gather.44
